TPU v7x, 512 devices: a whole 4x4x16 slice. The times are simulated.
512 devices in a mesh: rep: 32 (over z, core), row: 4 (over x), col: 4 (over y).
Axes of the slice: x: 4, y: 4, z: 16, core: 2. Of those that a mesh axis runs over, the one named last changes fastest.
Arguments:
- coordinates: bfloat16 [128, 32, 3, 128], P('rep')
- resample: int32 [32, 22], P('rep'), may hold values from 0 to 127, as said below
- block_slot: int32 [128], replicated, may hold values from 0 to 127, as said below
- lag_time: int32 [32], P('rep'), may hold values from 1 to 8
- atom_pairs: int32 [2, 4096], replicated, may hold values from 0 to 127, as said below
Outputs:
- instant_cov: bfloat16 [32, 4096, 4096], P('rep', 'row', 'col')
- lagged_cov: bfloat16 [32, 4096, 4096], P('rep', 'row', 'col')
Inputs may be any that keep to these rules, and one draw needn't show every extreme that they name: `resample`: the owner of a block is block_slot // 4. In each replicate at most 2 draws have one owner, and some owner has exactly 2; a block may be drawn more than once. `block_slot`: each slot holds exactly one block. `atom_pairs`: the two atoms of a feature differ, and no unordered pair of atoms appears twice.
All inputs are finite; a program needn't handle non-finite values.
Results may differ from a plain program's by a relative error of at most 0.0073.
Values may be sent and summed in bfloat16 or wider, within the bound.
No kernel may reach another device: no remote copies, remote signals or barrier semaphores. Data moves between devices by JAX's collectives and lax.ppermute only.
A program may use at most 64 MiB of HBM per device.

v0:
```python
import jax
import jax.numpy as jnp
from jax import lax
from jax.sharding import PartitionSpec as P

F = 4096
ATOMS = 128
BLOCK_LEN = 32
DRAWS = 22


def gather_blocks(coordinates, resample, block_slot):
    groups = lax.axis_size("row") * lax.axis_size("col")
    if BLOCK_LEN % groups:
        groups = 1
    frames = BLOCK_LEN // groups
    member = lax.axis_index("row") * lax.axis_size("col") + lax.axis_index("col")
    if groups == 1:
        member = 0
    piece = lax.dynamic_slice_in_dim(coordinates, member * frames, frames, axis=1)
    every = lax.all_gather(piece, "rep", axis=0, tiled=True)
    slots = jnp.take(block_slot, resample[0], axis=0)
    picked = jnp.take(every, slots, axis=0)
    if groups == 1:
        return picked
    return lax.all_gather(picked, ("row", "col"), axis=1, tiled=True)


def tile_features(chosen, atom_pairs, first_feature, width, shift):
    first_atoms = lax.dynamic_slice_in_dim(atom_pairs[0], first_feature, width)
    second_atoms = lax.dynamic_slice_in_dim(atom_pairs[1], first_feature, width)
    atom_ids = jnp.arange(chosen.shape[-1], dtype=jnp.int32)[:, None]
    signed = (
        (atom_ids == first_atoms[None, :]).astype(jnp.float32)
        - (atom_ids == second_atoms[None, :]).astype(jnp.float32)
    ).astype(jnp.bfloat16)
    flat = chosen.reshape(-1, chosen.shape[-1])
    difference = jnp.dot(flat, signed, preferred_element_type=jnp.float32).reshape(
        DRAWS, BLOCK_LEN, 3, width
    )
    squared = (
        difference[:, :, 0] * difference[:, :, 0]
        + difference[:, :, 1] * difference[:, :, 1]
        + difference[:, :, 2] * difference[:, :, 2]
    )
    features = jnp.sqrt(squared).astype(jnp.bfloat16)
    doubled = jnp.concatenate([features, features], axis=1)
    shifted = lax.dynamic_slice_in_dim(doubled, shift, BLOCK_LEN, axis=1)
    valid_rows = (jnp.arange(BLOCK_LEN, dtype=jnp.int32) < BLOCK_LEN - shift)[None, :, None]
    pair_count = (2 * DRAWS * (BLOCK_LEN - shift)).astype(jnp.float32)
    earlier = jnp.where(valid_rows, features.astype(jnp.float32), 0.0)
    later = jnp.where(valid_rows, shifted.astype(jnp.float32), 0.0)
    feature_mean = (jnp.sum(earlier, axis=(0, 1)) + jnp.sum(later, axis=(0, 1))) / pair_count
    zero_lag = (
        jnp.where(valid_rows, earlier - feature_mean, 0.0).astype(jnp.bfloat16).reshape(-1, width)
    )
    lagged = (
        jnp.where(valid_rows, later - feature_mean, 0.0).astype(jnp.bfloat16).reshape(-1, width)
    )
    return (zero_lag, lagged, pair_count)


def shards(coordinates, resample, block_slot, lag_time, atom_pairs):
    chosen = gather_blocks(coordinates, resample, block_slot)
    width = F // lax.axis_size("row")
    shift = lag_time[0]
    zero_row, lag_row, pair_count = tile_features(
        chosen, atom_pairs, lax.axis_index("row") * width, width, shift
    )
    row_stack = jnp.concatenate([zero_row, lag_row], axis=0)
    zero_col, lag_col, unused_count = tile_features(
        chosen, atom_pairs, lax.axis_index("col") * width, width, shift
    )
    col_stack = jnp.concatenate([zero_col, lag_col], axis=0)
    half_rows = col_stack.shape[0] // 2
    mirrored = jnp.concatenate([col_stack[half_rows:], col_stack[:half_rows]], axis=0)
    instant = (
        jnp.einsum("na,nb->ab", row_stack, col_stack, preferred_element_type=jnp.float32)
        / pair_count
    )
    crossed = (
        jnp.einsum("na,nb->ab", row_stack, mirrored, preferred_element_type=jnp.float32)
        / pair_count
    )
    return (instant[None].astype(jnp.bfloat16), crossed[None].astype(jnp.bfloat16))


def solution(mesh):
    return jax.shard_map(
        shards,
        mesh=mesh,
        in_specs=(P("rep", None, None, None), P("rep", None), P(), P("rep"), P()),
        out_specs=(P("rep", "row", "col"), P("rep", "row", "col")),
        check_vma=False,
    )
```

profile of v0, /device:TPU:2, one launch (start us, length us, event | category | flops | bytes accessed | tf_op | source)
XLA Modules:
  0.0 108.9 jit_solution(13588767077936588273)
XLA Ops:
  0.6 0.0 copy-start
  0.7 0.9 fusion.48
  1.6 0.0 copy-done
  1.6 36.8 %all_gather.6 = bf16[128,2,3,128]{3,1,2,0:T(2,128)(2,1)S(1)} all-gather(bf16[4,2,3,128]{3,1,2,0:T(2,128)(2,1)S(1)} %constant_dynamic-slice_fusion.4), channel_id=1, replica_groups=mesh['rep'=32,'row'=4,'col'=4] {'rep'}, dimensions={0}, use_global_device_ids=true | all-gather | bytes 202752 | tf_op jit(solution)/shard_map/all_gather | solution.py:21
  38.4 0.7 fusion.47
  39.0 1.4 %gather_fusion = s32[22]{0:T(128)S(1)} fusion(s32[128]{0:T(128)} %param.7, s32[1024]{0:T(1024)S(1)} %pad_clamp_fusion.1), kind=kCustom, calls=%fused_computation | custom fusion | bytes 264 | tf_op jit(solution)/shard_map/jit(_take)/gather | solution.py:22
  40.4 0.7 fusion.44
  41.1 0.6 gather_fusion.1
  41.7 0.7 compare_and_fusion
  42.4 0.1 broadcast_select_fusion
  42.5 24.1 %all_gather.7 = bf16[22,32,3,128]{3,0,2,1:T(8,128)(2,1)S(1)} all-gather(bf16[22,2,3,128]{3,0,2,1:T(8,128)(2,1)S(1)} %copy.13), channel_id=1, replica_groups=mesh['rep'=32,'row'=4,'col'=4] {'row','col'}, dimensions={1}, use_global_device_ids=true | all-gather | bytes 574464 | tf_op jit(solution)/shard_map/all_gather | solution.py:26
  66.6 1.3 %fusion.32 = f32[22,32,3,1024]{3,1,0,2:T(8,128)S(1)} fusion(bf16[22,32,3,128]{3,0,2,1:T(8,128)(2,1)S(1)} %all_gather.7, s32[1024]{0:T(1024)S(1)} %bitcast.60, s32[1024]{0:T(1024)S(1)} %bitcast.58), kind=kOutput, calls=%fused_computation.51 | convolution fusion | flops 554434560 | bytes 9199616 | tf_op jit(solution)/shard_map/dot_general | solution.py:38
  68.0 0.0 copy-start.1
  68.0 1.2 %fusion.49 = bf16[22,32,1024]{2,1,0:T(8,128)(2,1)S(1)} fusion(f32[22,32,3,1024]{3,1,0,2:T(8,128)S(1)} %fusion.32), kind=kLoop, calls=%fused_computation.90 | loop fusion | flops 4325376 | bytes 10092544 | tf_op jit(solution)/shard_map/sqrt | solution.py:46
  69.2 2.1 %copy-done.1 = f32[22,32,3,1024]{3,1,0,2:T(8,128)} copy-done((f32[22,32,3,1024]{3,1,0,2:T(8,128)}, f32[22,32,3,1024]{3,1,0,2:T(8,128)S(1)}, u32[]{:S(2)}) %copy-start.1) | copy-done | bytes 8650776
  71.3 1.3 %fusion.34 = f32[22,32,3,1024]{3,1,2,0:T(8,128)S(1)} fusion(bf16[22,32,3,128]{3,0,2,1:T(8,128)(2,1)S(1)} %all_gather.7, s32[1024]{0:T(1024)S(1)} %bitcast.59, s32[1024]{0:T(1024)S(1)} %bitcast.57), kind=kOutput, calls=%fused_computation.53 | convolution fusion | flops 554434560 | bytes 9199616 | tf_op jit(solution)/shard_map/dot_general | solution.py:38
  72.6 0.0 copy-start.2
  72.6 1.2 %fusion.50 = bf16[22,32,1024]{2,1,0:T(8,128)(2,1)S(1)} fusion(f32[22,32,3,1024]{3,1,2,0:T(8,128)S(1)} %fusion.34), kind=kLoop, calls=%fused_computation.91 | loop fusion | flops 4325376 | bytes 10092544 | tf_op jit(solution)/shard_map/sqrt | solution.py:46
  73.9 2.1 %copy-done.2 = f32[22,32,3,1024]{3,1,2,0:T(8,128)} copy-done((f32[22,32,3,1024]{3,1,2,0:T(8,128)}, f32[22,32,3,1024]{3,1,2,0:T(8,128)S(1)}, u32[]{:S(2)}) %copy-start.2) | copy-done | bytes 8650776
  76.6 8.7 %fusion.23 = (f32[1024]{0:T(1024)S(1)}, f32[1024]{0:T(1024)S(1)}, f32[1024]{0:T(1024)S(1)}, f32[1024]{0:T(1024)S(1)}) fusion(pred[32]{0:T(512)(128)(4,1)S(1)} %iota_compare_fusion.4, s32[]{:T(128)S(6)} %select_n.115, bf16[22,32,1024]{2,1,0:T(8,128)(2,1)S(1)} %fusion.50, bf16[22,32,1024]{2,1,0:T(8,128)(2,1)S(1)} %fusion.49, f32[22,32,3,1024]{3,1,0,2:T(8,128)} %copy-done.1, ...), kind=kLoop, calls=%fused_computation.45 | loop fusion | flops 21622784 | bytes 20201508 | tf_op jit(solution)/shard_map/reduce_sum | solution.py:53
  85.4 0.0 copy-start.3
  85.4 6.0 %fusion.2 = bf16[22,32,1,1024]{3,1,0,2:T(8,128)(2,1)} fusion(f32[22,32,3,1024]{3,1,0,2:T(8,128)} %copy-done.1), kind=kLoop, calls=%fused_computation.7 | loop fusion | flops 4325376 | bytes 10092544 | tf_op jit(solution)/shard_map/convert.1
  91.4 0.1 copy-done.3
  91.5 2.3 %fusion.6 = bf16[22,32,1,1024]{3,1,2,0:T(8,128)(2,1)} fusion(f32[22,32,3,1024]{3,1,2,0:T(8,128)S(1)} %copy-done.3), kind=kLoop, calls=%fused_computation.14 | loop fusion | flops 4325376 | bytes 10092544 | tf_op jit(solution)/shard_map/convert.3
  93.8 0.1 broadcast_in_dim.75
  93.9 3.1 %fusion.21 = (bf16[704,1024]{1,0:T(8,128)(2,1)S(1)}, bf16[704,1024]{1,0:T(8,128)(2,1)S(1)}) fusion(bf16[22,32,1,1024]{3,1,2,0:T(8,128)(2,1)} %fusion.6, f32[1024]{0:T(1024)S(1)} %get-tuple-element.17, pred[704]{0:T(1024)(128)(4,1)S(1)} %broadcast_in_dim.75, f32[1024]{0:T(1024)S(1)} %get-tuple-element.16, bf16[22,32,1,1024]{3,1,0,2:T(8,128)(2,1)} %fusion.2), kind=kLoop, calls=%fused_computation.38 | loop fusion | flops 7208960 | bytes 5776064 | tf_op jit(solution)/shard_map/convert_element_type | solution.py:55
  97.0 2.6 %select_convert_fusion.1 = (bf16[22,32,1024]{2,1,0:T(8,128)(2,1)S(1)}, bf16[22,32,1024]{2,1,0:T(8,128)(2,1)S(1)}) fusion(f32[1024]{0:T(1024)S(1)} %get-tuple-element.17, pred[32]{0:T(512)(128)(4,1)S(1)} %iota_compare_fusion.4, s32[]{:T(128)S(6)} %select_n.115, bf16[22,32,1024]{2,1,0:T(8,128)(2,1)S(1)} %fusion.50, f32[1024]{0:T(1024)S(1)} %get-tuple-element.16, ...), kind=kLoop, calls=%fused_computation.43 | loop fusion | flops 11534336 | bytes 5775396 | tf_op jit(solution)/shard_map/convert_element_type | solution.py:58
  99.6 4.7 %fusion.25 = bf16[1,1024,1024]{2,1,0:T(8,128)(2,1)} fusion(f32[]{:T(128)S(6)} %convert_element_type.76, bf16[704,1024]{1,0:T(8,128)(2,1)S(1)} %get-tuple-element.13, bf16[704,1024]{1,0:T(8,128)(2,1)S(1)} %bitcast.55, bf16[704,1024]{1,0:T(8,128)(2,1)S(1)} %bitcast.53, bf16[704,1024]{1,0:T(8,128)(2,1)S(1)} %get-tuple-element.12), kind=kOutput, calls=%fused_computation.48 | convolution fusion | flops 2966421504 | bytes 7864324 | tf_op jit(solution)/shard_map/na,nb->ab/dot_general | solution.py:82
  104.3 4.6 %fusion.24 = bf16[1,1024,1024]{2,1,0:T(8,128)(2,1)} fusion(f32[]{:T(128)S(6)} %convert_element_type.76, bf16[704,1024]{1,0:T(8,128)(2,1)S(1)} %bitcast.56, bf16[704,1024]{1,0:T(8,128)(2,1)S(1)} %get-tuple-element.13, bf16[704,1024]{1,0:T(8,128)(2,1)S(1)} %bitcast.54, bf16[704,1024]{1,0:T(8,128)(2,1)S(1)} %get-tuple-element.12), kind=kOutput, calls=%fused_computation.47 | convolution fusion | flops 2966421504 | bytes 7864324 | tf_op jit(solution)/shard_map/na,nb->ab/dot_general | solution.py:78
  (9 shorter events, 0.1 us)
Async XLA Ops:
  0.6 0.9 copy-start
  68.0 3.3 %copy-start.1 = (f32[22,32,3,1024]{3,1,0,2:T(8,128)}, f32[22,32,3,1024]{3,1,0,2:T(8,128)S(1)}, u32[]{:S(2)}) copy-start(f32[22,32,3,1024]{3,1,0,2:T(8,128)S(1)} %fusion.32) | copy-start | bytes 25952260
  72.6 3.3 %copy-start.2 = (f32[22,32,3,1024]{3,1,2,0:T(8,128)}, f32[22,32,3,1024]{3,1,2,0:T(8,128)S(1)}, u32[]{:S(2)}) copy-start(f32[22,32,3,1024]{3,1,2,0:T(8,128)S(1)} %fusion.34) | copy-start | bytes 25952260
  85.4 6.1 %copy-start.3 = (f32[22,32,3,1024]{3,1,2,0:T(8,128)S(1)}, f32[22,32,3,1024]{3,1,2,0:T(8,128)}, u32[]{:S(2)}) copy-start(f32[22,32,3,1024]{3,1,2,0:T(8,128)} %copy-done.2) | copy-start | bytes 25952260
where the time goes:
time: 109 us
  blocking collectives  60.9 us (56%)
  other arithmetic  27.3 us (25%)
  matrix products  11.9 us (11%)
  local copies, waits for them, and re-layouts  7.29 us (7%)
  between operations  1.46 us (1%)
    all_gather x1, blocking collectives, gather_blocks(): every = lax.all_gather(piece, 'rep', axis=0, tiled=True)  36.8 us
    all_gather x1, blocking collectives, gather_blocks(): return lax.all_gather(picked, ('row', 'col'), axis=1, tiled=True)  24.1 us
    reduce_sum x1, other arithmetic, tile_features(): jnp.sum(later, axis=(0, 1))  8.72 us
    another operation x2, other arithmetic  8.31 us
    dot_general x1, matrix products, shards(): jnp.einsum('na,nb->ab', row_stack, mirrored, preferred_element_type=jnp.f...  4.67 us
    dot_general x1, matrix products, shards(): jnp.einsum('na,nb->ab', row_stack, col_stack, preferred_element_type=jnp....  4.64 us
    unnamed x8, local copies, waits for them, and re-layouts  4.3 us
    convert_element_type x1, other arithmetic, tile_features(): jnp.where(valid_rows, earlier - feature_mean, 0.0).astype(jnp.bfloat16)  3.09 us

commit v1 on v0

--- a/solution.py
+++ b/solution.py
@@ -23,7 +23,10 @@
     picked = jnp.take(every, slots, axis=0)
     if groups == 1:
         return picked
-    return lax.all_gather(picked, ("row", "col"), axis=1, tiled=True)
+    return jnp.concatenate(
+        lax.all_to_all(jnp.stack([picked] * lax.axis_size(("row", "col"))), ("row", "col"), 0, 0),
+        axis=1,
+    )
 
 
 def tile_features(chosen, atom_pairs, first_feature, width, shift):

time: 109 us -> 87.9 us (0.81)
  the two profiles are of different devices: /device:TPU:2 before, /device:TPU:1 now
where the time goes in v1:
time: 87.9 us; the launch traced here: 87.5 us
  blocking collectives  38.1 us (43%)
  other arithmetic  16.2 us (18%)
  matrix products  11.9 us (14%)
  waiting for transfers between devices  8.68 us (10%)
  starting transfers between devices  6.75 us (8%)
  local copies, waits for them, and re-layouts  4.42 us (5%)
  between operations  1.42 us (2%)
    all_gather x1, blocking collectives, gather_blocks(): every = lax.all_gather(piece, 'rep', axis=0, tiled=True)  38.1 us
    all_to_all x1, waiting for transfers between devices, gather_blocks(): lax.all_to_all(jnp.stack([picked] * lax.axis_size(('row', 'col'))), ('row...  8.68 us
    all_to_all x1, starting transfers between devices, gather_blocks(): lax.all_to_all(jnp.stack([picked] * lax.axis_size(('row', 'col'))), ('row...  6.75 us
    reduce_sum x1, other arithmetic, tile_features(): jnp.sum(later, axis=(0, 1))  5.25 us
    dot_general x1, matrix products, shards(): jnp.einsum('na,nb->ab', row_stack, mirrored, preferred_element_type=jnp.f...  4.66 us
    dot_general x1, matrix products, shards(): jnp.einsum('na,nb->ab', row_stack, col_stack, preferred_element_type=jnp....  4.65 us
    convert_element_type x1, other arithmetic, tile_features(): jnp.where(valid_rows, later - feature_mean, 0.0).astype(jnp.bfloat16)  2.62 us
    dot_general x2, matrix products, tile_features(): jnp.dot(flat, signed, preferred_element_type=jnp.float32)  2.61 us
  transfers between devices with their start and end apart: 1, of which 1 were waited for; matrix products, arithmetic and copies ran while one was open for 1% of the time, Pallas kernels for 0%

profile of v1, /device:TPU:1, one launch (start us, length us, event | category | flops | bytes accessed | tf_op | source)
XLA Modules:
  0.0 87.5 jit_solution(13975090137176518192)
XLA Ops:
  0.6 0.0 copy-start
  0.6 0.7 fusion.46
  1.3 1.4 %gather_fusion = s32[22]{0:T(128)S(1)} fusion(s32[128]{0:T(128)} %param.7, s32[1024]{0:T(1024)S(1)} %pad_clamp_fusion.1), kind=kCustom, calls=%fused_computation | custom fusion | bytes 264 | tf_op jit(solution)/shard_map/jit(_take)/gather | solution.py:22
  2.7 0.7 fusion.43
  3.4 0.7 compare_and_fusion
  4.0 0.0 copy-done
  4.1 38.1 %all_gather.3 = bf16[128,2,3,128]{3,1,2,0:T(2,128)(2,1)S(1)} all-gather(bf16[4,2,3,128]{3,1,2,0:T(2,128)(2,1)S(1)} %constant_dynamic-slice_fusion.4), channel_id=1, replica_groups=mesh['rep'=32,'row'=4,'col'=4] {'rep'}, dimensions={0}, use_global_device_ids=true | all-gather | bytes 202752 | tf_op jit(solution)/shard_map/all_gather | solution.py:21
  42.2 0.6 gather_fusion.1
  42.8 0.1 broadcast_select_fusion
  42.9 1.1 %stack.2 = bf16[16,22,2,3,128]{4,2,3,1,0:T(2,128)(2,1)} broadcast(bf16[22,2,3,128]{3,1,2,0:T(2,128)(2,1)S(1)} %broadcast_select_fusion), dimensions={1,2,3,4} | broadcast | bytes 574464 | tf_op jit(solution)/shard_map/stack | solution.py:27
  44.0 6.8 %all-to-all-start = ((bf16[16,22,2,3,128]{4,2,3,1,0:T(2,128)(2,1)}), bf16[16,22,2,3,128]{4,2,3,1,0:T(2,128)(2,1)S(1)}, u32[]{:S(2)}, u32[]{:S(2)}) async-start(bf16[16,22,2,3,128]{4,2,3,1,0:T(2,128)(2,1)} %stack.2), calls=%async_computation | async-start | bytes 1081344 | tf_op jit(solution)/shard_map/all_to_all | solution.py:27
  50.8 0.9 fusion.47
  52.3 0.1 broadcast_in_dim.75
  52.4 8.7 %all-to-all-done = bf16[16,22,2,3,128]{4,2,3,1,0:T(2,128)(2,1)S(1)} async-done(((bf16[16,22,2,3,128]{4,2,3,1,0:T(2,128)(2,1)}), bf16[16,22,2,3,128]{4,2,3,1,0:T(2,128)(2,1)S(1)}, u32[]{:S(2)}, u32[]{:S(2)}) %all-to-all-start) | async-done | bytes 540704 | tf_op jit(solution)/shard_map/all_to_all | solution.py:27
  61.1 0.4 copy.13
  61.5 1.3 %fusion.32 = f32[22,32,3,1024]{3,1,0,2:T(8,128)S(1)} fusion(bf16[22,32,3,128]{3,1,2,0:T(8,128)(2,1)S(1)} %bitcast.56, s32[1024]{0:T(1024)S(1)} %bitcast.66, s32[1024]{0:T(1024)S(1)} %bitcast.65), kind=kOutput, calls=%fused_computation.51 | convolution fusion | flops 554434560 | bytes 9199616 | tf_op jit(solution)/shard_map/dot_general | solution.py:41
  62.8 1.2 %fusion.49 = bf16[22,32,1024]{2,1,0:T(8,128)(2,1)S(1)} fusion(f32[22,32,3,1024]{3,1,0,2:T(8,128)S(1)} %fusion.32), kind=kLoop, calls=%fused_computation.89 | loop fusion | flops 4325376 | bytes 10092544 | tf_op jit(solution)/shard_map/sqrt | solution.py:49
  64.0 1.2 %fusion.2 = bf16[22,32,1,1024]{3,1,0,2:T(8,128)(2,1)S(1)} fusion(f32[22,32,3,1024]{3,1,0,2:T(8,128)S(1)} %fusion.32), kind=kLoop, calls=%fused_computation.7 | loop fusion | flops 4325376 | bytes 10092544 | tf_op jit(solution)/shard_map/convert.1
  65.2 1.3 %fusion.35 = f32[22,32,3,1024]{3,1,2,0:T(8,128)S(1)} fusion(bf16[22,32,3,128]{3,1,2,0:T(8,128)(2,1)S(1)} %bitcast.57, s32[1024]{0:T(1024)S(1)} %bitcast.64, s32[1024]{0:T(1024)S(1)} %bitcast.63), kind=kOutput, calls=%fused_computation.60 | convolution fusion | flops 554434560 | bytes 9199616 | tf_op jit(solution)/shard_map/dot_general | solution.py:41
  66.5 1.2 %fusion.50 = bf16[22,32,1024]{2,1,0:T(8,128)(2,1)S(1)} fusion(f32[22,32,3,1024]{3,1,2,0:T(8,128)S(1)} %fusion.35), kind=kLoop, calls=%fused_computation.90 | loop fusion | flops 4325376 | bytes 10092544 | tf_op jit(solution)/shard_map/sqrt | solution.py:49
  67.7 1.2 %fusion.6 = bf16[22,32,1,1024]{3,1,2,0:T(8,128)(2,1)S(1)} fusion(f32[22,32,3,1024]{3,1,2,0:T(8,128)S(1)} %fusion.35), kind=kLoop, calls=%fused_computation.14 | loop fusion | flops 4325376 | bytes 10092544 | tf_op jit(solution)/shard_map/convert.3
  68.9 5.2 %fusion.23 = (f32[1024]{0:T(1024)S(1)}, f32[1024]{0:T(1024)S(1)}, f32[1024]{0:T(1024)S(1)}, f32[1024]{0:T(1024)S(1)}) fusion(pred[32]{0:T(512)(128)(4,1)S(1)} %iota_compare_fusion.4, s32[]{:T(128)S(6)} %select_n.117, bf16[22,32,1024]{2,1,0:T(8,128)(2,1)S(1)} %fusion.50, bf16[22,32,1024]{2,1,0:T(8,128)(2,1)S(1)} %fusion.49, ...), kind=kLoop, calls=%fused_computation.45 | loop fusion | flops 21622784 | bytes 20201508 | tf_op jit(solution)/shard_map/reduce_sum | solution.py:56
  74.2 2.6 %select_convert_fusion.1 = (bf16[22,32,1024]{2,1,0:T(8,128)(2,1)S(1)}, bf16[22,32,1024]{2,1,0:T(8,128)(2,1)S(1)}) fusion(f32[1024]{0:T(1024)S(1)} %get-tuple-element.17, pred[32]{0:T(512)(128)(4,1)S(1)} %iota_compare_fusion.4, s32[]{:T(128)S(6)} %select_n.117, bf16[22,32,1024]{2,1,0:T(8,128)(2,1)S(1)} %fusion.50, f32[1024]{0:T(1024)S(1)} %get-tuple-element.16, ...), kind=kLoop, calls=%fused_computation.43 | loop fusion | flops 11534336 | bytes 5775396 | tf_op jit(solution)/shard_map/convert_element_type | solution.py:61
  76.8 1.4 %fusion.21 = (bf16[704,1024]{1,0:T(8,128)(2,1)S(1)}, bf16[704,1024]{1,0:T(8,128)(2,1)S(1)}) fusion(bf16[22,32,1,1024]{3,1,2,0:T(8,128)(2,1)S(1)} %fusion.6, f32[1024]{0:T(1024)S(1)} %get-tuple-element.17, pred[704]{0:T(1024)(128)(4,1)S(1)} %broadcast_in_dim.75, f32[1024]{0:T(1024)S(1)} %get-tuple-element.16, bf16[22,32,1,1024]{3,1,0,2:T(8,128)(2,1)S(1)} %fusion.2), kind=kLoop, calls=%fused_computation.38 | loop fusion | flops 7208960 | bytes 5776064 | tf_op jit(solution)/shard_map/convert_element_type | solution.py:58
  78.2 4.7 %fusion.25 = bf16[1,1024,1024]{2,1,0:T(8,128)(2,1)} fusion(f32[]{:T(128)S(6)} %convert_element_type.76, bf16[704,1024]{1,0:T(8,128)(2,1)S(1)} %get-tuple-element.13, bf16[704,1024]{1,0:T(8,128)(2,1)S(1)} %bitcast.61, bf16[704,1024]{1,0:T(8,128)(2,1)S(1)} %bitcast.59, bf16[704,1024]{1,0:T(8,128)(2,1)S(1)} %get-tuple-element.12), kind=kOutput, calls=%fused_computation.48 | convolution fusion | flops 2966421504 | bytes 7864324 | tf_op jit(solution)/shard_map/na,nb->ab/dot_general | solution.py:85
  82.9 4.6 %fusion.24 = bf16[1,1024,1024]{2,1,0:T(8,128)(2,1)} fusion(f32[]{:T(128)S(6)} %convert_element_type.76, bf16[704,1024]{1,0:T(8,128)(2,1)S(1)} %bitcast.62, bf16[704,1024]{1,0:T(8,128)(2,1)S(1)} %get-tuple-element.13, bf16[704,1024]{1,0:T(8,128)(2,1)S(1)} %bitcast.60, bf16[704,1024]{1,0:T(8,128)(2,1)S(1)} %get-tuple-element.12), kind=kOutput, calls=%fused_computation.47 | convolution fusion | flops 2966421504 | bytes 7864324 | tf_op jit(solution)/shard_map/na,nb->ab/dot_general | solution.py:81
  (8 shorter events, 0.1 us)
Async XLA Ops:
  0.6 3.4 %copy-start = (bf16[4,32,3,128]{3,1,2,0:T(8,128)(2,1)S(1)}, bf16[4,32,3,128]{3,1,2,0:T(8,128)(2,1)}, u32[]{:S(2)}) copy-start(bf16[4,32,3,128]{3,1,2,0:T(8,128)(2,1)} %param.5) | copy-start | bytes 294916
  44.0 17.1 %all-to-all-start = ((bf16[16,22,2,3,128]{4,2,3,1,0:T(2,128)(2,1)}), bf16[16,22,2,3,128]{4,2,3,1,0:T(2,128)(2,1)S(1)}, u32[]{:S(2)}, u32[]{:S(2)}) async-start(bf16[16,22,2,3,128]{4,2,3,1,0:T(2,128)(2,1)} %stack.2), calls=%async_computation | async-start | bytes 1081344 | tf_op jit(solution)/shard_map/all_to_all | solution.py:27
